TPU v7x, 256 devices: a whole 4x4x8 slice. The times are simulated.
256 devices in a mesh: dp: 4 (over y), head: 4 (over x), seq: 16 (over z, core).
Axes of the slice: x: 4, y: 4, z: 8, core: 2. Of those that a mesh axis runs over, the one named last changes fastest.
Arguments:
- q_dense: bfloat16 [32768, 8, 128], P(('dp', 'seq'), 'head'), parts along dimension 0, may hold values from -108 to 108
- k_dense: bfloat16 [32768, 8, 128], P(('dp', 'seq'), 'head'), parts along dimension 0, may hold values from -4 to 4
- v_dense: bfloat16 [32768, 8, 128], P(('dp', 'seq'), 'head'), parts along dimension 0, may hold values from -4 to 4
- q_expert: bfloat16 [32768, 12, 128], P(('dp', 'seq'), 'head'), parts along dimension 0, may hold values from -108 to 108
- k_expert: bfloat16 [32768, 12, 128], P(('dp', 'seq'), 'head'), parts along dimension 0, may hold values from -4 to 4
- v_expert: bfloat16 [32768, 12, 128], P(('dp', 'seq'), 'head'), parts along dimension 0, may hold values from -4 to 4
- gate_logit: bfloat16 [12, 32768], P('head', ('dp', 'seq')), parts along dimension 1, may hold values from -8 to 8
- selection: int32 [12, 2048], P('head', 'dp'), parts along dimension 1, may hold values from 0 to 8191, as said below
Outputs:
- dense_out: bfloat16 [32768, 8, 128], P(('dp', 'seq'), 'head'), parts along dimension 0
- expert_out: bfloat16 [32768, 12, 128], P(('dp', 'seq'), 'head'), parts along dimension 0
There are 4 independent parts, one for each index of `dp`. A program takes and returns all parts, laid end to end along the dimension named above; each array names one. Nothing has to cross between parts.
Inputs may be any that keep to these rules, and one draw needn't show every extreme that they name: `selection`: each row lists 512 distinct token positions in increasing order; every row holds the first and the last token.
All inputs are finite; a program needn't handle non-finite values.
Results may differ from a plain program's by a relative error of at most 0.0055.
Values may be sent and summed in bfloat16 or wider, within the bound.
No kernel may reach another device: no remote copies, remote signals or barrier semaphores. Data moves between devices by JAX's collectives and lax.ppermute only.
A program may use at most 64 MiB of HBM per device.

v0:
```python
import math
import jax
import jax.numpy as jnp
from jax import lax
from jax.sharding import PartitionSpec as P

NEGATIVE = -1e30


def plain_rows(rows, tok_rows, count):
    return rows


def online_update(state, queries, query_pos, keys, values, key_pos, scale):
    leading, total, summed = state
    scores = jnp.einsum("qhd,khd->qhk", queries, keys, preferred_element_type=jnp.float32) * scale
    visible = key_pos[None, None, :] <= query_pos[:, None, None]
    scores = jnp.where(visible, scores, NEGATIVE)
    new_leading = jnp.maximum(leading, jnp.max(scores, axis=2))
    shrink = jnp.exp(leading - new_leading)
    weights = jnp.where(visible, jnp.exp(scores - new_leading[:, :, None]), 0.0)
    total = total * shrink + jnp.sum(weights, axis=2)
    moved = jnp.einsum(
        "qhk,khd->qhd", weights.astype(jnp.bfloat16), values, preferred_element_type=jnp.float32
    )
    return (new_leading, total, summed * shrink[:, :, None] + moved)


def dense_heads(queries, keys, values, position_map):
    tok_rows, heads, width = queries.shape
    count = lax.axis_size("seq")
    half_rows = tok_rows // 2
    own_rows = lax.axis_index("seq") * tok_rows + jnp.arange(tok_rows, dtype=jnp.int32)
    query_pos = position_map(own_rows, tok_rows, count).reshape(2, half_rows)
    groups = queries.reshape(2, half_rows, heads, width)
    scale = 1.0 / math.sqrt(width)
    blank = (
        jnp.full((half_rows, heads), NEGATIVE, jnp.float32),
        jnp.zeros((half_rows, heads), jnp.float32),
        jnp.zeros((half_rows, heads, width), jnp.float32),
    )
    key_rows = lax.all_gather(keys, "seq", axis=0, tiled=True)
    value_rows = lax.all_gather(values, "seq", axis=0, tiled=True)
    length = key_rows.shape[0]
    block = math.gcd(length, 512)
    count_blocks = length // block
    key_pos = position_map(jnp.arange(length, dtype=jnp.int32), tok_rows, count).reshape(
        count_blocks, block
    )
    key_blocks = key_rows.reshape(count_blocks, block, heads, width)
    value_blocks = value_rows.reshape(count_blocks, block, heads, width)

    def advance(state, item):
        key_block, value_block, block_pos = item
        result = []
        for group in range(2):
            seen = jnp.min(block_pos) <= jnp.max(query_pos[group])
            result.append(
                lax.cond(
                    seen,
                    lambda inner, member=group: online_update(
                        inner,
                        groups[member],
                        query_pos[member],
                        key_block,
                        value_block,
                        block_pos,
                        scale,
                    ),
                    lambda inner: inner,
                    state[group],
                )
            )
        return (tuple(result), None)

    final_state, unused = lax.scan(advance, (blank, blank), (key_blocks, value_blocks, key_pos))
    outputs = [
        (summed / total[:, :, None]).astype(jnp.bfloat16) for leading, total, summed in final_state
    ]
    return jnp.concatenate(outputs, axis=0)


def attend_ranked(query_rows, query_ranks, keys, values, gate_rows):
    heads, rows, width = query_rows.shape
    block = math.gcd(rows, 512)
    scale = 1.0 / math.sqrt(width)
    key_ranks = jnp.arange(keys.shape[1], dtype=jnp.int32)

    def one_block(index):
        scores = (
            jnp.einsum("erd,ekd->erk", query_rows, keys, preferred_element_type=jnp.float32) * scale
        )
        visible = key_ranks[None, None, :] <= query_ranks[:, :, None]
        scores = jnp.where(visible, scores, NEGATIVE)
        leading = jnp.max(scores, axis=2, keepdims=True)
        weights = jnp.where(visible, jnp.exp(scores - leading), 0.0)
        total = jnp.sum(weights, axis=2, keepdims=True)
        mixed = (
            jnp.einsum(
                "erk,ekd->erd",
                weights.astype(jnp.bfloat16),
                values,
                preferred_element_type=jnp.float32,
            )
            / total
        )
        return (mixed * jax.nn.sigmoid(gate_rows.astype(jnp.float32))[:, :, None]).astype(
            jnp.bfloat16
        )

    blocks = lax.map(one_block, jnp.arange(rows // block, dtype=jnp.int32))
    return jnp.moveaxis(blocks, 0, 1).reshape(heads, rows, width)


def sparse_heads(queries, keys, values, gate_logit, selection):
    tok_rows, heads, width = queries.shape
    chosen = selection.shape[1]
    start = lax.axis_index("seq") * tok_rows
    positions = start + jnp.arange(tok_rows, dtype=jnp.int32)
    matches = selection[:, :, None] == positions[None, None, :]
    one_hot = matches.astype(jnp.bfloat16)

    def pick(source):
        return jnp.einsum(
            "ent,ted->end", one_hot, source, preferred_element_type=jnp.float32
        ).astype(jnp.bfloat16)

    gate_rows = jnp.einsum("ent,et->en", one_hot, gate_logit, preferred_element_type=jnp.float32)
    gathered = (
        lax.psum(pick(queries), "seq").astype(jnp.float32),
        lax.psum(pick(keys), "seq").astype(jnp.float32),
        lax.psum(pick(values), "seq").astype(jnp.float32),
        lax.psum(gate_rows.astype(jnp.bfloat16), "seq").astype(jnp.float32),
    )
    picked_q, picked_k, picked_v, picked_gate = [member.astype(jnp.bfloat16) for member in gathered]
    all_ranks = jnp.broadcast_to(jnp.arange(chosen, dtype=jnp.int32)[None, :], (heads, chosen))
    results = attend_ranked(picked_q, all_ranks, picked_k, picked_v, picked_gate)
    return jnp.einsum("ent,end->ted", one_hot, results, preferred_element_type=jnp.float32).astype(
        jnp.bfloat16
    )


def local(q_dense, k_dense, v_dense, q_expert, k_expert, v_expert, gate_logit, selection):
    dense_out = dense_heads(q_dense, k_dense, v_dense, plain_rows)
    expert_out = sparse_heads(q_expert, k_expert, v_expert, gate_logit, selection)
    return (dense_out, expert_out)


def solution(mesh):
    placed = (
        P(("dp", "seq"), "head", None),
        P(("dp", "seq"), "head", None),
        P(("dp", "seq"), "head", None),
        P(("dp", "seq"), "head", None),
        P(("dp", "seq"), "head", None),
        P(("dp", "seq"), "head", None),
        P("head", ("dp", "seq")),
        P("head", "dp"),
    )
    return jax.shard_map(
        local,
        mesh=mesh,
        in_specs=placed,
        out_specs=(P(("dp", "seq"), "head", None), P(("dp", "seq"), "head", None)),
        check_vma=False,
    )
```

profile of v0, /device:TPU:225, one launch (start us, length us, event | category | flops | bytes accessed | tf_op | source)
XLA Modules:
  0.0 332.1 jit_solution(16076033150022781153)
XLA Ops:
  8.2 2.1 fusion.67
  10.3 2.5 fusion.61
  12.7 1.4 fusion.64
  16.6 23.1 %psum.31 = bf16[3,512]{1,0:T(4,128)(2,1)S(1)} all-reduce(bf16[3,512]{1,0:T(4,128)(2,1)S(1)} %bitcast.68), channel_id=1, replica_groups=mesh['dp'=4,'head'=4,'seq'=16] {'seq'}, use_global_device_ids=true, to_apply=%region_18.19 | all-reduce | flops 1536 | bytes 6144 | tf_op jit(solution)/shard_map/psum | solution.py:133
  40.3 87.0 %all-reduce.3.cloned.1.call-done = (bf16[3,512,128]{2,1,0:T(8,128)(2,1)}, bf16[3,512,128]{2,1,0:T(8,128)(2,1)}, bf16[3,512,128]{2,1,0:T(8,128)(2,1)}) async-done(((bf16[3,512,128]{2,1,0:T(8,128)(2,1)}, bf16[3,512,128]{2,1,0:T(8,128)(2,1)}, bf16[3,512,128]{2,1,0:T(8,128)(2,1)}), (bf16[3,512,128]{2,1,0:T(8,128)(2,1)}, bf16[3,512,128]{2,1,0:T(8,128)(2,1)}, ...) | async-done | bytes 1179664 | tf_op jit(solution)/shard_map/psum | solution.py:132
  127.3 2.1 fusion.90
  129.5 1.6 fusion.73
  132.0 39.2 %all-gather.3.cloned.1.call-done = bf16[8192,2,128]{2,0,1:T(8,128)(2,1)} async-done(((bf16[512,2,128]{2,0,1:T(8,128)(2,1)}), bf16[8192,2,128]{2,0,1:T(8,128)(2,1)}) %all-gather.3.cloned.1.call-update) | async-done | bytes 4194320 | tf_op jit(solution)/shard_map/all_gather | solution.py:42
  171.2 42.6 %all-gather.5.cloned.1.call-done = bf16[8192,2,128]{2,0,1:T(8,128)(2,1)} async-done(((bf16[512,2,128]{2,0,1:T(8,128)(2,1)}), bf16[8192,2,128]{2,0,1:T(8,128)(2,1)}) %all-gather.5.cloned.1.call-update) | async-done | bytes 4194320 | tf_op jit(solution)/shard_map/all_gather | solution.py:43
  213.9 109.1 %while.26 = (s32[]{:T(128)}, f32[256,2]{0,1:T(2,128)S(1)}, f32[256,2]{0,1:T(2,128)S(1)}, f32[256,2,128]{2,0,1:T(8,128)S(1)}, f32[256,2]{0,1:T(2,128)S(1)}, /*ind...) while((s32[]{:T(128)}, f32[256,2]{0,1:T(2,128)S(1)}, ...), condition=%wide.region_12.13_spmd.clone, body=%wide.region_2.12_spmd.clone.sunk | while | flops 273682432 | bytes 10830257 | solution.py:76
  215.9 1.1 dynamic-slice_bitcast_fusion.3
  217.0 1.3 conditional.6
  219.4 1.3 conditional.7
  222.7 1.1 dynamic-slice_bitcast_fusion.3
  223.8 1.3 conditional.6
  226.3 1.3 conditional.7
  229.5 1.1 dynamic-slice_bitcast_fusion.3
  230.6 1.3 conditional.6
  233.1 1.3 conditional.7
  236.3 1.1 dynamic-slice_bitcast_fusion.3
  237.4 1.3 conditional.6
  239.9 1.3 conditional.7
  244.2 1.3 conditional.6
  246.7 1.3 conditional.7
  250.0 1.1 dynamic-slice_bitcast_fusion.3
  251.0 1.3 conditional.6
  253.5 1.3 conditional.7
  257.9 1.3 conditional.6
  260.3 1.3 conditional.7
  264.7 1.3 conditional.6
  267.2 1.3 conditional.7
  271.5 1.3 conditional.6
  274.0 1.3 conditional.7
  278.3 1.3 conditional.6
  280.8 1.3 conditional.7
  285.1 1.3 conditional.6
  287.6 1.3 conditional.7
  291.9 1.3 conditional.6
  294.4 1.3 conditional.7
  298.8 1.3 conditional.6
  301.2 1.3 conditional.7
  305.6 1.3 conditional.6
  308.1 1.3 conditional.7
  312.4 1.3 conditional.6
  314.9 1.3 conditional.7
  319.2 1.3 conditional.6
  321.7 1.3 conditional.7
  323.3 1.2 fusion.82
  (341 shorter events, 67.6 us)
Async XLA Ops:
  7.2 1.0 copy-start
  7.2 5.6 %copy-start.6 = (s32[3,512]{1,0:T(4,128)S(1)}, s32[3,512]{1,0:T(4,128)}, u32[]{:S(2)}) copy-start(s32[3,512]{1,0:T(4,128)} %param.21) | copy-start | bytes 18436
  7.2 5.5 %copy-start.4 = (bf16[512,3,128]{2,0,1:T(8,128)(2,1)S(1)}, bf16[512,3,128]{2,0,1:T(8,128)(2,1)}, u32[]{:S(2)}) copy-start(bf16[512,3,128]{2,0,1:T(8,128)(2,1)} %param.18) | copy-start | bytes 1179652
  7.2 120.1 %all-reduce.3.cloned.1.call-start = ((), (), s32[]{:S(2)}) async-start(), calls=%async_computation.2 | async-start | bytes 2359296 | tf_op jit(solution)/shard_map/psum | solution.py:132
  10.3 4.0 %copy-start.1 = (bf16[512,2,128]{2,1,0:T(2,128)(2,1)S(1)}, bf16[512,2,128]{2,1,0:T(2,128)(2,1)}, u32[]{:S(2)}) copy-start(bf16[512,2,128]{2,1,0:T(2,128)(2,1)} %param.15) | copy-start | bytes 786436
  10.3 4.8 %copy-start.2 = (bf16[512,2,128]{2,1,0:T(2,128)(2,1)S(1)}, bf16[512,2,128]{2,1,0:T(2,128)(2,1)}, u32[]{:S(2)}) copy-start(bf16[512,2,128]{2,1,0:T(2,128)(2,1)} %param.16) | copy-start | bytes 786436
  10.3 5.6 %copy-start.3 = (bf16[512,2,128]{2,1,0:T(2,128)(2,1)S(1)}, bf16[512,2,128]{2,1,0:T(2,128)(2,1)}, u32[]{:S(2)}) copy-start(bf16[512,2,128]{2,1,0:T(2,128)(2,1)} %param.14) | copy-start | bytes 786436
  12.7 3.2 copy-start.7
  14.2 157.1 %all-gather.3.cloned.1.call-start = ((), (), s32[]{:S(2)}) async-start(), calls=%async_computation | async-start | bytes 4456448 | tf_op jit(solution)/shard_map/all_gather | solution.py:42
  15.0 198.9 %all-gather.5.cloned.1.call-start = ((), (), s32[]{:S(2)}) async-start(), calls=%async_computation.1 | async-start | bytes 4456448 | tf_op jit(solution)/shard_map/all_gather | solution.py:43
  127.3 2.1 copy-start.5
Sparse Core Ops, SparseCore 0:
  14.3 113.0 all-reduce.2
  129.8 41.4 all-gather.2
  173.1 40.6 all-gather.4
where the time goes:
time: 333 us; the launch traced here: 332 us
  waiting for transfers between devices  169 us (51%)
  loops' own time  42.3 us (13%)
  matrix products  36.9 us (11%)
  other arithmetic  25.7 us (8%)
  blocking collectives  23.1 us (7%)
  local copies, waits for them, and re-layouts  21.1 us (6%)
  between operations  13.9 us (4%)
    psum x1, waiting for transfers between devices, sparse_heads(): lax.psum(pick(values), 'seq').astype(jnp.float32)  87 us
    all_gather x1, waiting for transfers between devices, dense_heads(): value_rows = lax.all_gather(values, 'seq', axis=0, tiled=True)  42.6 us
    another operation x1, loops' own time, dense_heads(): lax.scan(advance, (blank, blank), (key_blocks, value_blocks, key_pos))  40.4 us
    all_gather x1, waiting for transfers between devices, dense_heads(): key_rows = lax.all_gather(keys, 'seq', axis=0, tiled=True)  39.2 us
    psum x1, blocking collectives, sparse_heads(): lax.psum(gate_rows.astype(jnp.bfloat16), 'seq').astype(jnp.float32)  23.1 us
    squeeze x16, local copies, waits for them, and re-layouts, dense_heads(): lax.scan(advance, (blank, blank), (key_blocks, value_blocks, key_pos))  17.2 us
    dot_general x32, matrix products, online_update(): jnp.einsum('qhk,khd->qhd', weights.astype(jnp.bfloat16), values, preferre...  16.5 us
    reduce_min x16, other arithmetic, advance(): seen = jnp.min(block_pos) <= jnp.max(query_pos[group])  10.3 us
  transfers between devices with their start and end apart: 3, of which 3 were waited for; matrix products, arithmetic and copies ran while one was open for 2% of the time, Pallas kernels for 0%

commit v1 on v0

--- a/solution.py
+++ b/solution.py
@@ -39,7 +39,11 @@
         jnp.zeros((half_rows, heads), jnp.float32),
         jnp.zeros((half_rows, heads, width), jnp.float32),
     )
-    key_rows = lax.all_gather(keys, "seq", axis=0, tiled=True)
+    devices = lax.axis_size("seq")
+    repeats = [devices if d == 0 else 1 for d in range(keys.ndim)]
+    key_rows = lax.all_to_all(
+        jnp.tile(keys, repeats), "seq", split_axis=0, concat_axis=0, tiled=True
+    )
     value_rows = lax.all_gather(values, "seq", axis=0, tiled=True)
     length = key_rows.shape[0]
     block = math.gcd(length, 512)

time: 333 us -> 365 us (1.096)
  blocking collectives: 23.1 us -> 113 us
  waiting for transfers between devices: 169 us -> 81.3 us
  local copies, waits for them, and re-layouts: 21.1 us -> 42.8 us
  starting transfers between devices: 0.12 us -> 6.38 us
    psum x1, blocking collectives: 23.1 us -> 113 us  [sparse_heads(): lax.psum(gate_rows.astype(jnp.bfloat16), 'seq').astype(jnp.float32)]
    psum x1, waiting for transfers between devices: 87 us -> 42 us  [sparse_heads(): lax.psum(pick(values), 'seq').astype(jnp.float32)]
    all_gather x1 -> x0, waiting for transfers between devices: 39.2 us -> none  [dense_heads(): key_rows = lax.all_gather(keys, 'seq', axis=0, tiled=True)]
    dynamic_slice x0 -> x32, local copies, waits for them, and re-layouts: none -> 18.8 us  [dense_heads(): lax.scan(advance, (blank, blank), (key_blocks, value_blocks, key_pos))]
    all_to_all x0 -> x1, starting transfers between devices: none -> 6.31 us  [dense_heads(): lax.all_to_all(jnp.tile(keys, repeats), 'seq', split_axis=0, concat_axis=...]
    another operation x0 -> x1, local copies, waits for them, and re-layouts: none -> 5.21 us  [dense_heads(): jnp.tile(keys, repeats)]
  transfers between devices with their start and end apart: 3 -> 3, of which waited for: 3 -> 2; matrix products, arithmetic and copies ran while one was open for 2% -> 3% of each run, Pallas kernels for 0% -> 0%
where the time goes in v1:
time: 365 us; the launch traced here: 363 us
  blocking collectives  113 us (31%)
  waiting for transfers between devices  81.3 us (22%)
  loops' own time  43.2 us (12%)
  local copies, waits for them, and re-layouts  42.8 us (12%)
  matrix products  36.9 us (10%)
  other arithmetic  25.7 us (7%)
  between operations  14.2 us (4%)
  starting transfers between devices  6.38 us (2%)
    psum x1, blocking collectives, sparse_heads(): lax.psum(gate_rows.astype(jnp.bfloat16), 'seq').astype(jnp.float32)  113 us
    psum x1, waiting for transfers between devices, sparse_heads(): lax.psum(pick(values), 'seq').astype(jnp.float32)  42 us
    another operation x1, loops' own time, dense_heads(): lax.scan(advance, (blank, blank), (key_blocks, value_blocks, key_pos))  41.3 us
    all_gather x1, waiting for transfers between devices, dense_heads(): value_rows = lax.all_gather(values, 'seq', axis=0, tiled=True)  39.3 us
    dynamic_slice x32, local copies, waits for them, and re-layouts, dense_heads(): lax.scan(advance, (blank, blank), (key_blocks, value_blocks, key_pos))  18.8 us
    dot_general x32, matrix products, online_update(): jnp.einsum('qhk,khd->qhd', weights.astype(jnp.bfloat16), values, preferre...  16.5 us
    squeeze x16, local copies, waits for them, and re-layouts, dense_heads(): lax.scan(advance, (blank, blank), (key_blocks, value_blocks, key_pos))  15.7 us
    reduce_min x16, other arithmetic, advance(): seen = jnp.min(block_pos) <= jnp.max(query_pos[group])  10.3 us
  transfers between devices with their start and end apart: 3, of which 2 were waited for; matrix products, arithmetic and copies ran while one was open for 3% of the time, Pallas kernels for 0%

profile of v1, /device:TPU:225, one launch (start us, length us, event | category | flops | bytes accessed | tf_op | source)
XLA Modules:
  0.0 363.5 jit_solution(12181003370883493377)
XLA Ops:
  8.2 2.1 fusion.67
  10.3 2.4 fusion.61
  12.7 1.4 fusion.64
  14.1 5.2 %tile.4 = bf16[16,512,2,128]{3,2,1,0:T(2,128)(2,1)} broadcast(bf16[512,2,128]{2,1,0:T(2,128)(2,1)S(1)} %copy-done.1), dimensions={1,2,3} | broadcast | bytes 4456448 | tf_op jit(solution)/shard_map/tile | solution.py:45
  19.3 6.3 %all-to-all-start = ((bf16[8192,2,128]{2,1,0:T(2,128)(2,1)}), bf16[8192,2,128]{2,1,0:T(2,128)(2,1)}, u32[]{:S(2)}, u32[]{:S(2)}) async-start(bf16[8192,2,128]{2,1,0:T(2,128)(2,1)} %bitcast.63), calls=%async_computation | async-start | bytes 8388608 | tf_op jit(solution)/shard_map/all_to_all | solution.py:44
  27.2 113.0 %psum.31 = bf16[3,512]{1,0:T(4,128)(2,1)S(1)} all-reduce(bf16[3,512]{1,0:T(4,128)(2,1)S(1)} %bitcast.72), channel_id=1, replica_groups=mesh['dp'=4,'head'=4,'seq'=16] {'seq'}, use_global_device_ids=true, to_apply=%region_18.19 | all-reduce | flops 1536 | bytes 6144 | tf_op jit(solution)/shard_map/psum | solution.py:137
  140.9 42.0 %all-reduce.3.cloned.1.call-done = (bf16[3,512,128]{2,1,0:T(8,128)(2,1)}, bf16[3,512,128]{2,1,0:T(8,128)(2,1)}, bf16[3,512,128]{2,1,0:T(8,128)(2,1)}) async-done(((bf16[3,512,128]{2,1,0:T(8,128)(2,1)}, bf16[3,512,128]{2,1,0:T(8,128)(2,1)}, bf16[3,512,128]{2,1,0:T(8,128)(2,1)}), (bf16[3,512,128]{2,1,0:T(8,128)(2,1)}, bf16[3,512,128]{2,1,0:T(8,128)(2,1)}, ...) | async-done | bytes 1179664 | tf_op jit(solution)/shard_map/psum | solution.py:136
  182.8 2.1 fusion.90
  185.0 1.6 fusion.73
  187.5 39.3 %all-gather.2.cloned.1.call-done = bf16[8192,2,128]{2,0,1:T(8,128)(2,1)} async-done(((bf16[512,2,128]{2,0,1:T(8,128)(2,1)}), bf16[8192,2,128]{2,0,1:T(8,128)(2,1)}) %all-gather.2.cloned.1.call-update) | async-done | bytes 4194320 | tf_op jit(solution)/shard_map/all_gather | solution.py:47
  226.9 127.2 %while.26 = (s32[]{:T(128)}, f32[256,2]{0,1:T(2,128)S(1)}, f32[256,2]{0,1:T(2,128)S(1)}, f32[256,2,128]{2,0,1:T(8,128)S(1)}, f32[256,2]{0,1:T(2,128)S(1)}, /*ind...) while((s32[]{:T(128)}, f32[256,2]{0,1:T(2,128)S(1)}, ...), condition=%wide.region_12.13_spmd.clone, body=%wide.region_2.12_spmd.clone.sunk | while | flops 273682432 | bytes 11354549 | solution.py:80
  228.8 1.1 constant_dynamic-slice_fusion.4
  231.0 1.3 conditional.6
  233.5 1.3 conditional.7
  236.7 1.1 constant_dynamic-slice_fusion.4
  238.9 1.3 conditional.6
  241.5 1.3 conditional.7
  244.7 1.1 constant_dynamic-slice_fusion.4
  246.9 1.3 conditional.6
  249.4 1.3 conditional.7
  252.6 1.1 constant_dynamic-slice_fusion.4
  254.8 1.3 conditional.6
  257.4 1.3 conditional.7
  262.8 1.3 conditional.6
  265.3 1.3 conditional.7
  270.7 1.3 conditional.6
  273.3 1.3 conditional.7
  278.7 1.3 conditional.6
  281.2 1.3 conditional.7
  286.6 1.3 conditional.6
  289.2 1.3 conditional.7
  294.6 1.3 conditional.6
  297.1 1.3 conditional.7
  302.5 1.3 conditional.6
  305.1 1.3 conditional.7
  310.5 1.3 conditional.6
  313.0 1.3 conditional.7
  318.4 1.3 conditional.6
  321.0 1.3 conditional.7
  326.4 1.3 conditional.6
  328.9 1.3 conditional.7
  334.3 1.3 conditional.6
  336.9 1.3 conditional.7
  342.3 1.3 conditional.6
  344.8 1.3 conditional.7
  350.2 1.3 conditional.6
  352.8 1.3 conditional.7
  354.3 1.2 fusion.82
  (372 shorter events, 84.9 us)
Async XLA Ops:
  7.2 1.0 copy-start
  7.2 5.5 %copy-start.6 = (s32[3,512]{1,0:T(4,128)S(1)}, s32[3,512]{1,0:T(4,128)}, u32[]{:S(2)}) copy-start(s32[3,512]{1,0:T(4,128)} %param.21) | copy-start | bytes 18436
  7.2 5.5 %copy-start.4 = (bf16[512,3,128]{2,0,1:T(8,128)(2,1)S(1)}, bf16[512,3,128]{2,0,1:T(8,128)(2,1)}, u32[]{:S(2)}) copy-start(bf16[512,3,128]{2,0,1:T(8,128)(2,1)} %param.18) | copy-start | bytes 1179652
  7.2 175.6 %all-reduce.3.cloned.1.call-start = ((), (), s32[]{:S(2)}) async-start(), calls=%async_computation.2 | async-start | bytes 2359296 | tf_op jit(solution)/shard_map/psum | solution.py:136
  10.3 3.9 %copy-start.1 = (bf16[512,2,128]{2,1,0:T(2,128)(2,1)S(1)}, bf16[512,2,128]{2,1,0:T(2,128)(2,1)}, u32[]{:S(2)}) copy-start(bf16[512,2,128]{2,1,0:T(2,128)(2,1)} %param.15) | copy-start | bytes 786436
  19.3 6.4 %copy-start.2 = (bf16[512,2,128]{2,1,0:T(2,128)(2,1)S(1)}, bf16[512,2,128]{2,1,0:T(2,128)(2,1)}, u32[]{:S(2)}) copy-start(bf16[512,2,128]{2,1,0:T(2,128)(2,1)} %param.16) | copy-start | bytes 786436
  19.3 7.1 %copy-start.3 = (bf16[512,2,128]{2,1,0:T(2,128)(2,1)S(1)}, bf16[512,2,128]{2,1,0:T(2,128)(2,1)}, u32[]{:S(2)}) copy-start(bf16[512,2,128]{2,1,0:T(2,128)(2,1)} %param.14) | copy-start | bytes 786436
  19.3 7.2 %copy-start.7 = (bf16[3,512]{1,0:T(4,128)(2,1)S(1)}, bf16[3,512]{1,0:T(4,128)(2,1)}, u32[]{:S(2)}) copy-start(bf16[3,512]{1,0:T(4,128)(2,1)} %param.20) | copy-start | bytes 9220
  19.3 168.2 %all-to-all-start = ((bf16[8192,2,128]{2,1,0:T(2,128)(2,1)}), bf16[8192,2,128]{2,1,0:T(2,128)(2,1)}, u32[]{:S(2)}, u32[]{:S(2)}) async-start(bf16[8192,2,128]{2,1,0:T(2,128)(2,1)} %bitcast.63), calls=%async_computation | async-start | bytes 8388608 | tf_op jit(solution)/shard_map/all_to_all | solution.py:44
  25.6 201.1 %all-gather.2.cloned.1.call-start = ((), (), s32[]{:S(2)}) async-start(), calls=%async_computation.1 | async-start | bytes 4456448 | tf_op jit(solution)/shard_map/all_gather | solution.py:47
  182.8 2.1 copy-start.5
Sparse Core Ops, SparseCore 0:
  14.2 168.5 all-reduce.2
  185.3 41.4 all-gather.1
